TPU v7x, 256 devices: a whole 4x4x8 slice. The times are simulated.
256 devices in a mesh: chan: 64 (over z, y_lo, x), ma: 4 (over y_hi, core).
Axes of the slice: x: 4, y: 4 (y_hi: 2, y_lo: 2; y = y_hi * 2 + y_lo), z: 8, core: 2. Of those that a mesh axis runs over, the one named last changes fastest.
Arguments:
- beam_table: bfloat16 [512, 1024, 2048], P(('ma', 'chan')), parts along dimension 0, may hold values from -0.125 to 0.125
- covariance: bfloat16 [8192, 128, 128], P(('ma', 'chan')), parts along dimension 0, as said below
- noise_var: float32 [512, 512], P(('ma', 'chan')), parts along dimension 0, may hold values from 0.5 to 4
- start_field: float32 [512, 512, 256], P(('ma', 'chan')), parts along dimension 0, may hold values from -4 to 4
- probes: float32 [512, 512, 256], P(('ma', 'chan')), parts along dimension 0, may hold values from -6 to 6
Outputs:
- solved: float32 [512, 512, 256], P(('ma', 'chan')), parts along dimension 0
- multipole_band_power: bfloat16 [8192, 128, 128], P(('ma', 'chan')), parts along dimension 0
There are 4 independent parts, one for each index of `ma`. A program takes and returns all parts, laid end to end along the dimension named above; each array names one. Nothing has to cross between parts.
Inputs may be any that keep to these rules, and one draw needn't show every extreme that they name: Each covariance[l] is symmetric with diagonal entries between 1 and 2.
All inputs are finite; a program needn't handle non-finite values.
Results may differ from a plain program's by a relative error of at most 0.009.
Values may be sent and summed in bfloat16 or wider, within the bound.
No kernel may reach another device: no remote copies, remote signals or barrier semaphores. Data moves between devices by JAX's collectives and lax.ppermute only.
A program may use at most 128 MiB of HBM per device.

v0:
```python
import jax
import jax.numpy as jnp
from jax import lax
from jax.sharding import PartitionSpec as P

ITERS = 2
WEIGHT = 0.2


def project_back(beam_table, field_b):
    column_entries = field_b.shape[2] // 2
    reals = field_b[:, :, :column_entries]
    imags = field_b[:, :, column_entries:]
    lower = jnp.concatenate([imags, -reals], axis=2)
    stacked = jnp.concatenate([field_b, lower], axis=1)
    return jnp.einsum("fkl,fkc->flc", beam_table, stacked, preferred_element_type=jnp.float32)


def project_out(beam_table, mixed_back):
    column_entries = mixed_back.shape[2] // 2
    modes = beam_table.shape[1] // 2
    product = jnp.einsum("fkl,flc->fkc", beam_table, mixed_back, preferred_element_type=jnp.float32)
    upper = product[:, :modes]
    lower = product[:, modes:]
    return jnp.concatenate(
        [
            upper[:, :, :column_entries] - lower[:, :, column_entries:],
            upper[:, :, column_entries:] + lower[:, :, :column_entries],
        ],
        axis=2,
    )


def apply_operator(beam_table, covariance, field):
    field_b = field.astype(jnp.bfloat16)
    sky_map = project_back(beam_table, field_b).astype(jnp.bfloat16)
    channel_mixed = jnp.einsum(
        "drj,jdi->rdi",
        covariance,
        lax.all_to_all(sky_map, "chan", split_axis=1, concat_axis=0, tiled=True),
        preferred_element_type=jnp.float32,
    )
    mixed_back = lax.all_to_all(
        channel_mixed.astype(jnp.bfloat16), "chan", split_axis=0, concat_axis=1, tiled=True
    )
    return project_out(beam_table, mixed_back)


def on_device(beam_table, covariance, noise_var, start_field, probes):
    field = start_field
    column_entries = field.shape[2] // 2
    for repeat in range(ITERS):
        image = apply_operator(beam_table, covariance, field)
        field = field + WEIGHT * (probes - image - noise_var[:, :, None] * field)
    final_sky = project_back(beam_table, field.astype(jnp.bfloat16)).astype(jnp.bfloat16)
    collected_parts = lax.all_to_all(final_sky, "chan", split_axis=1, concat_axis=0, tiled=True)
    multipole_band_power = (
        jnp.einsum(
            "mjk,ujk->jmu", collected_parts, collected_parts, preferred_element_type=jnp.float32
        )
        / column_entries
    )
    return (field, multipole_band_power.astype(jnp.bfloat16))


def solution(mesh):
    return jax.shard_map(
        on_device,
        mesh=mesh,
        in_specs=(
            P(("ma", "chan"), None, None),
            P(("ma", "chan"), None, None),
            P(("ma", "chan"), None),
            P(("ma", "chan"), None, None),
            P(("ma", "chan"), None, None),
        ),
        out_specs=(P(("ma", "chan"), None, None), P(("ma", "chan"), None, None)),
        check_vma=False,
    )
```

profile of v0, /device:TPU:2, one launch (start us, length us, event | category | flops | bytes accessed | tf_op | source)
XLA Modules:
  0.0 362.9 jit_solution(1768359897878251081)
XLA Ops:
  0.6 1.6 copy.48
  2.4 7.2 %fusion = bf16[2,2048,256]{1,2,0:T(8,128)(2,1)} fusion(bf16[2,1024,2048]{2,1,0:T(8,128)(2,1)} %param.5, bf16[2,512,128]{1,2,0:T(8,128)(2,1)S(1)} %get-tuple-element.19, bf16[2,512,128]{1,2,0:T(8,128)(2,1)S(1)} %get-tuple-element.18, bf16[2,512,256]{1,2,0:T(8,128)(2,1)S(1)} %convert_element_type.42), kind=kOutput, calls=%fused_computation.3 | convolution fusion | flops 2151677952 | bytes 11534336 | tf_op jit(solution)/shard_map/fkl,fkc->flc/dot_general | solution.py:16
  9.6 6.1 %copy.39 = bf16[2,2048,256]{2,0,1:T(2,128)(2,1)} copy(bf16[2,2048,256]{1,2,0:T(8,128)(2,1)} %fusion) | data formatting | bytes 4194304 | tf_op jit(solution)/shard_map/convert_element_type | solution.py:36
  15.7 63.4 %all_to_all.90 = bf16[2,2048,256]{2,0,1:T(2,128)(2,1)S(1)} all-to-all(bf16[2,2048,256]{2,0,1:T(2,128)(2,1)} %copy.39), channel_id=1, replica_groups=mesh['chan'=64,'ma'=4] {'chan'}, dimensions={1} | all-to-all | bytes 4194304 | tf_op jit(solution)/shard_map/all_to_all | solution.py:40
  79.2 0.3 copy.40
  79.6 3.0 convert_bitcast_fusion.1
  82.6 4.6 %copy.43 = bf16[128,32,256]{2,1,0:T(8,128)(2,1)} copy(bf16[128,32,256]{0,2,1:T(8,128)(2,1)} %convert_bitcast_fusion.1) | data formatting | bytes 4194304 | tf_op jit(solution)/shard_map/convert_element_type | solution.py:44
  87.2 7.1 %all-to-all-start.1 = ((bf16[128,32,256]{2,1,0:T(8,128)(2,1)}), bf16[128,32,256]{2,1,0:T(8,128)(2,1)}, u32[]{:S(2)}, u32[]{:S(2)}) async-start(bf16[128,32,256]{2,1,0:T(8,128)(2,1)} %copy.43), calls=%async_computation.1 | async-start | bytes 4194304 | tf_op jit(solution)/shard_map/all_to_all | solution.py:43
  94.3 1.6 copy.46
  95.8 47.6 %all-to-all-done.1 = bf16[128,32,256]{2,1,0:T(8,128)(2,1)} async-done(((bf16[128,32,256]{2,1,0:T(8,128)(2,1)}), bf16[128,32,256]{2,1,0:T(8,128)(2,1)}, u32[]{:S(2)}, u32[]{:S(2)}) %all-to-all-start.1) | async-done | bytes 2097184 | tf_op jit(solution)/shard_map/all_to_all | solution.py:43
  143.5 1.9 copy.44
  145.4 6.2 %convolution_bitcast_fusion.1 = f32[2,1024,256]{1,2,0:T(8,128)S(1)} fusion(bf16[2,2048,256]{2,1,0:T(8,128)(2,1)S(1)} %bitcast.52, bf16[2,1024,2048]{2,1,0:T(8,128)(2,1)} %param.5), kind=kOutput, calls=%fused_computation.14 | convolution fusion | flops 2147483648 | bytes 12582912 | tf_op jit(solution)/shard_map/fkl,flc->fkc/dot_general | solution.py:22
  151.9 0.4 copy-done.7
  152.3 0.4 fusion.32
  152.8 3.8 %fusion.1 = bf16[2,2048,256]{1,2,0:T(8,128)(2,1)} fusion(bf16[2,1024,2048]{2,1,0:T(8,128)(2,1)S(1)} %bitcast.55, bf16[2,512,128]{1,2,0:T(8,128)(2,1)S(1)} %get-tuple-element.17, bf16[2,512,128]{1,2,0:T(8,128)(2,1)S(1)} %get-tuple-element.16, bf16[2,512,256]{1,2,0:T(8,128)(2,1)S(1)} %fusion.32), kind=kOutput, calls=%fused_computation.4 | convolution fusion | flops 2151677952 | bytes 11534336 | tf_op jit(solution)/shard_map/fkl,fkc->flc/dot_general | solution.py:16
  156.7 6.1 %copy.49 = bf16[2,2048,256]{2,0,1:T(2,128)(2,1)} copy(bf16[2,2048,256]{1,2,0:T(8,128)(2,1)} %fusion.1) | data formatting | bytes 4194304 | tf_op jit(solution)/shard_map/convert_element_type | solution.py:36
  162.8 56.1 %all_to_all.91 = bf16[2,2048,256]{2,0,1:T(2,128)(2,1)S(1)} all-to-all(bf16[2,2048,256]{2,0,1:T(2,128)(2,1)} %copy.49), channel_id=1, replica_groups=mesh['chan'=64,'ma'=4] {'chan'}, dimensions={1} | all-to-all | bytes 4194304 | tf_op jit(solution)/shard_map/all_to_all | solution.py:40
  218.9 0.3 copy.50
  219.3 3.0 convert_bitcast_fusion
  222.3 4.5 %copy.53 = bf16[128,32,256]{2,1,0:T(8,128)(2,1)} copy(bf16[128,32,256]{0,2,1:T(8,128)(2,1)} %convert_bitcast_fusion) | data formatting | bytes 4194304 | tf_op jit(solution)/shard_map/convert_element_type | solution.py:44
  226.9 56.0 %all_to_all.92 = bf16[128,32,256]{2,1,0:T(8,128)(2,1)S(1)} all-to-all(bf16[128,32,256]{2,1,0:T(8,128)(2,1)} %copy.53), channel_id=1, replica_groups=mesh['chan'=64,'ma'=4] {'chan'}, dimensions={0} | all-to-all | bytes 4194304 | tf_op jit(solution)/shard_map/all_to_all | solution.py:43
  283.1 6.2 %convolution_bitcast_fusion = f32[2,1024,256]{1,2,0:T(8,128)S(1)} fusion(bf16[2,2048,256]{2,1,0:T(8,128)(2,1)S(1)} %bitcast.53, bf16[2,1024,2048]{2,1,0:T(8,128)(2,1)} %param.5), kind=kOutput, calls=%fused_computation.13 | convolution fusion | flops 2147483648 | bytes 12582912 | tf_op jit(solution)/shard_map/fkl,flc->fkc/dot_general | solution.py:22
  289.6 0.8 copy-done.3
  290.6 1.5 fusion.36
  292.1 2.5 fusion.2
  294.6 3.8 %copy.57 = bf16[2,2048,256]{2,0,1:T(2,128)(2,1)} copy(bf16[2,2048,256]{1,2,0:T(8,128)(2,1)S(1)} %fusion.2) | data formatting | bytes 4194304 | tf_op jit(solution)/shard_map/convert_element_type | solution.py:55
  298.5 7.0 %all-to-all-start.4 = ((bf16[2,2048,256]{2,0,1:T(2,128)(2,1)}), bf16[2,2048,256]{2,0,1:T(2,128)(2,1)S(1)}, u32[]{:S(2)}, u32[]{:S(2)}) async-start(bf16[2,2048,256]{2,0,1:T(2,128)(2,1)} %copy.57), calls=%async_computation.4 | async-start | bytes 4194304 | tf_op jit(solution)/shard_map/all_to_all | solution.py:56
  305.5 1.3 copy.60
  306.8 47.8 %all-to-all-done.4 = bf16[2,2048,256]{2,0,1:T(2,128)(2,1)S(1)} async-done(((bf16[2,2048,256]{2,0,1:T(2,128)(2,1)}), bf16[2,2048,256]{2,0,1:T(2,128)(2,1)S(1)}, u32[]{:S(2)}, u32[]{:S(2)}) %all-to-all-start.4) | async-done | bytes 2097184 | tf_op jit(solution)/shard_map/all_to_all | solution.py:56
  354.9 3.5 copy.59
  358.4 2.8 all_to_all.84
  361.2 1.7 multiply_convert_fusion
  (34 shorter events, 1.7 us)
Async XLA Ops:
  0.6 79.0 %copy-start = (bf16[32,128,128]{2,1,0:T(8,128)(2,1)S(1)}, bf16[32,128,128]{2,1,0:T(8,128)(2,1)}, u32[]{:S(2)}) copy-start(bf16[32,128,128]{2,1,0:T(8,128)(2,1)} %param.6) | copy-start | bytes 3145732
  87.2 56.3 %all-to-all-start.1 = ((bf16[128,32,256]{2,1,0:T(8,128)(2,1)}), bf16[128,32,256]{2,1,0:T(8,128)(2,1)}, u32[]{:S(2)}, u32[]{:S(2)}) async-start(bf16[128,32,256]{2,1,0:T(8,128)(2,1)} %copy.43), calls=%async_computation.1 | async-start | bytes 4194304 | tf_op jit(solution)/shard_map/all_to_all | solution.py:43
  143.5 9.4 %slice-start = ((s8[8388608]{0:T(1024)(128)(4,1)}), s8[4194304]{0:T(1024)(128)(4,1)S(1)}, s32[]{:S(2)}) async-start(s8[8388608]{0:T(1024)(128)(4,1)} %bitcast.54), calls=%async_computation.5 | async-start | bytes 8388608
  145.4 7.4 %slice-start.1 = ((s8[8388608]{0:T(1024)(128)(4,1)}), s8[4194304]{0:T(1024)(128)(4,1)S(1)}, s32[]{:S(2)}) async-start(s8[8388608]{0:T(1024)(128)(4,1)} %bitcast.54), calls=%async_computation.6 | async-start | bytes 8388608
  151.6 0.7 copy-start.7
  151.9 0.9 copy-start.2
  151.9 1.0 copy-start.4
  282.9 9.2 %slice-start.2 = ((s8[8388608]{0:T(1024)(128)(4,1)}), s8[4194304]{0:T(1024)(128)(4,1)S(1)}, s32[]{:S(2)}) async-start(s8[8388608]{0:T(1024)(128)(4,1)} %bitcast.56), calls=%async_computation.7 | async-start | bytes 8388608
  283.1 9.0 %slice-start.3 = ((s8[8388608]{0:T(1024)(128)(4,1)}), s8[4194304]{0:T(1024)(128)(4,1)S(1)}, s32[]{:S(2)}) async-start(s8[8388608]{0:T(1024)(128)(4,1)} %bitcast.56), calls=%async_computation.8 | async-start | bytes 8388608
  289.4 1.0 copy-start.3
  289.4 1.2 copy-start.5
  298.5 7.0 %copy-start.6 = (f32[2,512,256]{1,2,0:T(8,128)S(1)}, f32[2,512,256]{1,2,0:T(8,128)}, u32[]{:S(2)}) copy-start(f32[2,512,256]{1,2,0:T(8,128)} %get-tuple-element.9) | copy-start | bytes 3145732
  298.5 56.1 %all-to-all-start.4 = ((bf16[2,2048,256]{2,0,1:T(2,128)(2,1)}), bf16[2,2048,256]{2,0,1:T(2,128)(2,1)S(1)}, u32[]{:S(2)}, u32[]{:S(2)}) async-start(bf16[2,2048,256]{2,0,1:T(2,128)(2,1)} %copy.57), calls=%async_computation.4 | async-start | bytes 4194304 | tf_op jit(solution)/shard_map/all_to_all | solution.py:56
  358.4 4.5 %copy-start.1 = (bf16[32,128,128]{2,1,0:T(8,128)(2,1)S(1)}, bf16[32,128,128]{2,1,0:T(8,128)(2,1)}, u32[]{:S(2)}) copy-start(bf16[32,128,128]{2,1,0:T(8,128)(2,1)} %param.6) | copy-start | bytes 3145732
where the time goes:
time: 364 us; the launch traced here: 363 us
  blocking collectives  176 us (48%)
  waiting for transfers between devices  95.4 us (26%)
  local copies, waits for them, and re-layouts  40.8 us (11%)
  matrix products  33.6 us (9%)
  starting transfers between devices  14 us (4%)
    all_to_all x2, blocking collectives, apply_operator(): lax.all_to_all(sky_map, 'chan', split_axis=1, concat_axis=0, tiled=True)  119 us
    all_to_all x1, blocking collectives, apply_operator(): lax.all_to_all(channel_mixed.astype(jnp.bfloat16), 'chan', split_axis=0,...  56 us
    all_to_all x1, waiting for transfers between devices, on_device(): lax.all_to_all(final_sky, 'chan', split_axis=1, concat_axis=0, tiled=True)  47.8 us
    all_to_all x1, waiting for transfers between devices, apply_operator(): lax.all_to_all(channel_mixed.astype(jnp.bfloat16), 'chan', split_axis=0,...  47.6 us
    dot_general x3, matrix products, project_back(): jnp.einsum('fkl,fkc->flc', beam_table, stacked, preferred_element_type=jn...  13.5 us
    dot_general x2, matrix products, project_out(): jnp.einsum('fkl,flc->fkc', beam_table, mixed_back, preferred_element_type...  12.4 us
    convert_element_type x2, local copies, waits for them, and re-layouts, apply_operator(): sky_map = project_back(beam_table, field_b).astype(jnp.bfloat16)  12.2 us
    convert_element_type x2, local copies, waits for them, and re-layouts, apply_operator(): channel_mixed.astype(jnp.bfloat16)  9.14 us
  transfers between devices with their start and end apart: 2, of which 2 were waited for; matrix products, arithmetic and copies ran while one was open for 1% of the time, Pallas kernels for 0%

commit v1 on v0

--- a/solution.py
+++ b/solution.py
@@ -53,7 +53,12 @@
         image = apply_operator(beam_table, covariance, field)
         field = field + WEIGHT * (probes - image - noise_var[:, :, None] * field)
     final_sky = project_back(beam_table, field.astype(jnp.bfloat16)).astype(jnp.bfloat16)
-    collected_parts = lax.all_to_all(final_sky, "chan", split_axis=1, concat_axis=0, tiled=True)
+    collected_parts = jnp.concatenate(
+        lax.all_to_all(
+            jnp.stack(jnp.split(final_sky, lax.axis_size("chan"), axis=1)), "chan", 0, 0
+        ),
+        axis=0,
+    )
     multipole_band_power = (
         jnp.einsum(
             "mjk,ujk->jmu", collected_parts, collected_parts, preferred_element_type=jnp.float32

time: 364 us -> 467 us (1.28)
  local copies, waits for them, and re-layouts: 40.8 us -> 140 us
    another operation x0 -> x69, local copies, waits for them, and re-layouts: none -> 60.4 us  [on_device(): jnp.stack(jnp.split(final_sky, lax.axis_size('chan'), axis=1))]
    unnamed x27 -> x150, local copies, waits for them, and re-layouts: 6.02 us -> 54.9 us
    all_to_all x3 -> x0, local copies, waits for them, and re-layouts: 6.6 us -> none  [on_device(): lax.all_to_all(final_sky, 'chan', split_axis=1, concat_axis=0, tiled=True)]
where the time goes in v1:
time: 467 us; the launch traced here: 464 us
  blocking collectives  175 us (37%)
  local copies, waits for them, and re-layouts  140 us (30%)
  waiting for transfers between devices  95.4 us (20%)
  matrix products  35.4 us (8%)
  starting transfers between devices  14.3 us (3%)
    all_to_all x2, blocking collectives, apply_operator(): lax.all_to_all(sky_map, 'chan', split_axis=1, concat_axis=0, tiled=True)  119 us
    another operation x69, local copies, waits for them, and re-layouts, on_device(): jnp.stack(jnp.split(final_sky, lax.axis_size('chan'), axis=1))  60.4 us
    all_to_all x1, blocking collectives, apply_operator(): lax.all_to_all(channel_mixed.astype(jnp.bfloat16), 'chan', split_axis=0,...  56 us
    unnamed x150, local copies, waits for them, and re-layouts  54.9 us
    all_to_all x1, waiting for transfers between devices, on_device(): lax.all_to_all(jnp.stack(jnp.split(final_sky, lax.axis_size('chan'), axis...  47.8 us
    all_to_all x1, waiting for transfers between devices, apply_operator(): lax.all_to_all(channel_mixed.astype(jnp.bfloat16), 'chan', split_axis=0,...  47.6 us
    dot_general x3, matrix products, project_back(): jnp.einsum('fkl,fkc->flc', beam_table, stacked, preferred_element_type=jn...  13.5 us
    dot_general x2, matrix products, project_out(): jnp.einsum('fkl,flc->fkc', beam_table, mixed_back, preferred_element_type...  12.4 us
  transfers between devices with their start and end apart: 2, of which 2 were waited for; matrix products, arithmetic and copies ran while one was open for 1% of the time, Pallas kernels for 0%

profile of v1, /device:TPU:2, one launch (start us, length us, event | category | flops | bytes accessed | tf_op | source)
XLA Modules:
  0.0 464.3 jit_solution(5602822884990466275)
XLA Ops:
  0.6 1.6 copy.49
  2.4 7.2 %fusion = bf16[2,2048,256]{1,2,0:T(8,128)(2,1)} fusion(bf16[2,1024,2048]{2,1,0:T(8,128)(2,1)} %param.5, bf16[2,512,128]{1,2,0:T(8,128)(2,1)S(1)} %get-tuple-element.83, bf16[2,512,128]{1,2,0:T(8,128)(2,1)S(1)} %get-tuple-element.82, bf16[2,512,256]{1,2,0:T(8,128)(2,1)S(1)} %convert_element_type.42), kind=kOutput, calls=%fused_computation.3 | convolution fusion | flops 2151677952 | bytes 11534336 | tf_op jit(solution)/shard_map/fkl,fkc->flc/dot_general | solution.py:16
  9.6 6.2 %copy.40 = bf16[2,2048,256]{2,0,1:T(2,128)(2,1)} copy(bf16[2,2048,256]{1,2,0:T(8,128)(2,1)} %fusion) | data formatting | bytes 4194304 | tf_op jit(solution)/shard_map/convert_element_type | solution.py:36
  15.8 63.4 %all_to_all.77 = bf16[2,2048,256]{2,0,1:T(2,128)(2,1)S(1)} all-to-all(bf16[2,2048,256]{2,0,1:T(2,128)(2,1)} %copy.40), channel_id=1, replica_groups=mesh['chan'=64,'ma'=4] {'chan'}, dimensions={1} | all-to-all | bytes 4194304 | tf_op jit(solution)/shard_map/all_to_all | solution.py:40
  79.7 3.0 convert_bitcast_fusion.1
  82.7 4.6 copy.44
  87.3 7.1 %all-to-all-start.1 = ((bf16[128,32,256]{2,1,0:T(8,128)(2,1)}), bf16[128,32,256]{2,1,0:T(8,128)(2,1)}, u32[]{:S(2)}, u32[]{:S(2)}) async-start(bf16[128,32,256]{2,1,0:T(8,128)(2,1)} %copy.44), calls=%async_computation.1 | async-start | bytes 4194304 | tf_op jit(solution)/shard_map/all_to_all | solution.py:43
  95.9 47.6 %all-to-all-done.1 = bf16[128,32,256]{2,1,0:T(8,128)(2,1)} async-done(((bf16[128,32,256]{2,1,0:T(8,128)(2,1)}), bf16[128,32,256]{2,1,0:T(8,128)(2,1)}, u32[]{:S(2)}, u32[]{:S(2)}) %all-to-all-start.1) | async-done | bytes 2097184 | tf_op jit(solution)/shard_map/all_to_all | solution.py:43
  143.6 1.9 copy.45
  145.5 6.2 %convolution_bitcast_fusion.1 = f32[2,1024,256]{1,2,0:T(8,128)S(1)} fusion(bf16[2,2048,256]{2,1,0:T(8,128)(2,1)S(1)} %bitcast.174, bf16[2,1024,2048]{2,1,0:T(8,128)(2,1)} %param.5), kind=kOutput, calls=%fused_computation.16 | convolution fusion | flops 2147483648 | bytes 12582912 | tf_op jit(solution)/shard_map/fkl,flc->fkc/dot_general | solution.py:22
  152.9 3.8 fusion.1
  156.8 6.2 %copy.50 = bf16[2,2048,256]{2,0,1:T(2,128)(2,1)} copy(bf16[2,2048,256]{1,2,0:T(8,128)(2,1)} %fusion.1) | data formatting | bytes 4194304 | tf_op jit(solution)/shard_map/convert_element_type | solution.py:36
  162.9 56.1 %all_to_all.78 = bf16[2,2048,256]{2,0,1:T(2,128)(2,1)S(1)} all-to-all(bf16[2,2048,256]{2,0,1:T(2,128)(2,1)} %copy.50), channel_id=1, replica_groups=mesh['chan'=64,'ma'=4] {'chan'}, dimensions={1} | all-to-all | bytes 4194304 | tf_op jit(solution)/shard_map/all_to_all | solution.py:40
  219.5 3.0 convert_bitcast_fusion
  222.5 4.6 copy.54
  227.1 56.0 %all_to_all.79 = bf16[128,32,256]{2,1,0:T(8,128)(2,1)S(1)} all-to-all(bf16[128,32,256]{2,1,0:T(8,128)(2,1)} %copy.54), channel_id=1, replica_groups=mesh['chan'=64,'ma'=4] {'chan'}, dimensions={0} | all-to-all | bytes 4194304 | tf_op jit(solution)/shard_map/all_to_all | solution.py:43
  283.3 6.2 %convolution_bitcast_fusion = f32[2,1024,256]{1,2,0:T(8,128)S(1)} fusion(bf16[2,2048,256]{2,1,0:T(8,128)(2,1)S(1)} %bitcast.175, bf16[2,1024,2048]{2,1,0:T(8,128)(2,1)} %param.5), kind=kOutput, calls=%fused_computation.15 | convolution fusion | flops 2147483648 | bytes 12582912 | tf_op jit(solution)/shard_map/fkl,flc->fkc/dot_general | solution.py:22
  292.3 2.4 fusion.2
  295.0 2.0 slice_bitcast_fusion.38
  297.0 2.0 slice_bitcast_fusion
  312.5 1.6 copy.78
  314.1 1.6 copy.77
  315.7 1.6 copy.76
  317.4 1.6 copy.75
  319.0 1.6 copy.74
  320.6 1.6 copy.73
  322.2 1.6 copy.72
  328.6 1.6 copy.68
  333.4 1.6 copy.65
  404.5 7.2 %all-to-all-start.4 = ((bf16[64,2,32,256]{3,2,1,0:T(8,128)(2,1)}), bf16[64,2,32,256]{3,2,1,0:T(8,128)(2,1)S(1)}, u32[]{:S(2)}, u32[]{:S(2)}) async-start(bf16[64,2,32,256]{3,2,1,0:T(8,128)(2,1)} %constant_dynamic-update-slice_fusion), calls=%async_computation.4 | async-start | bytes 4194304 | tf_op jit(solution)/shard_map/all_to_all | solution.py:57
  413.1 47.8 %all-to-all-done.4 = bf16[64,2,32,256]{3,2,1,0:T(8,128)(2,1)S(1)} async-done(((bf16[64,2,32,256]{3,2,1,0:T(8,128)(2,1)}), bf16[64,2,32,256]{3,2,1,0:T(8,128)(2,1)S(1)}, u32[]{:S(2)}, u32[]{:S(2)}) %all-to-all-start.4) | async-done | bytes 2097184 | tf_op jit(solution)/shard_map/all_to_all | solution.py:57
  460.9 3.4 multiply_convert_fusion
  (222 shorter events, 98.6 us)
Async XLA Ops:
  0.6 79.0 %copy-start = (bf16[32,128,128]{2,1,0:T(8,128)(2,1)S(1)}, bf16[32,128,128]{2,1,0:T(8,128)(2,1)}, u32[]{:S(2)}) copy-start(bf16[32,128,128]{2,1,0:T(8,128)(2,1)} %param.6) | copy-start | bytes 3145732
  87.3 56.2 %all-to-all-start.1 = ((bf16[128,32,256]{2,1,0:T(8,128)(2,1)}), bf16[128,32,256]{2,1,0:T(8,128)(2,1)}, u32[]{:S(2)}, u32[]{:S(2)}) async-start(bf16[128,32,256]{2,1,0:T(8,128)(2,1)} %copy.44), calls=%async_computation.1 | async-start | bytes 4194304 | tf_op jit(solution)/shard_map/all_to_all | solution.py:43
  312.5 39.9 %copy-start.13 = (bf16[1,2,32,256]{2,3,1,0:T(8,128)(2,1)S(1)}, bf16[1,2,32,256]{2,3,1,0:T(8,128)(2,1)}, u32[]{:S(2)}) copy-start(bf16[1,2,32,256]{2,3,1,0:T(8,128)(2,1)} %get-tuple-element.21) | copy-start | bytes 98308
  314.1 39.0 %copy-start.12 = (bf16[1,2,32,256]{2,3,1,0:T(8,128)(2,1)S(1)}, bf16[1,2,32,256]{2,3,1,0:T(8,128)(2,1)}, u32[]{:S(2)}) copy-start(bf16[1,2,32,256]{2,3,1,0:T(8,128)(2,1)} %get-tuple-element.22) | copy-start | bytes 98308
  315.7 37.4 %copy-start.11 = (bf16[1,2,32,256]{2,3,1,0:T(8,128)(2,1)S(1)}, bf16[1,2,32,256]{2,3,1,0:T(8,128)(2,1)}, u32[]{:S(2)}) copy-start(bf16[1,2,32,256]{2,3,1,0:T(8,128)(2,1)} %get-tuple-element.23) | copy-start | bytes 98308
  317.4 35.9 %copy-start.10 = (bf16[1,2,32,256]{2,3,1,0:T(8,128)(2,1)S(1)}, bf16[1,2,32,256]{2,3,1,0:T(8,128)(2,1)}, u32[]{:S(2)}) copy-start(bf16[1,2,32,256]{2,3,1,0:T(8,128)(2,1)} %get-tuple-element.24) | copy-start | bytes 98308
  319.0 34.4 %copy-start.9 = (bf16[1,2,32,256]{2,3,1,0:T(8,128)(2,1)S(1)}, bf16[1,2,32,256]{2,3,1,0:T(8,128)(2,1)}, u32[]{:S(2)}) copy-start(bf16[1,2,32,256]{2,3,1,0:T(8,128)(2,1)} %get-tuple-element.25) | copy-start | bytes 98308
  320.6 32.9 %copy-start.8 = (bf16[1,2,32,256]{2,3,1,0:T(8,128)(2,1)S(1)}, bf16[1,2,32,256]{2,3,1,0:T(8,128)(2,1)}, u32[]{:S(2)}) copy-start(bf16[1,2,32,256]{2,3,1,0:T(8,128)(2,1)} %get-tuple-element.26) | copy-start | bytes 98308
  322.2 31.3 %copy-start.7 = (bf16[1,2,32,256]{2,3,1,0:T(8,128)(2,1)S(1)}, bf16[1,2,32,256]{2,3,1,0:T(8,128)(2,1)}, u32[]{:S(2)}) copy-start(bf16[1,2,32,256]{2,3,1,0:T(8,128)(2,1)} %get-tuple-element.27) | copy-start | bytes 98308
  353.8 21.6 %copy-start.35 = (bf16[1,2,32,256]{3,2,1,0:T(8,128)(2,1)S(1)}, bf16[1,2,32,256]{3,2,1,0:T(8,128)(2,1)}, u32[]{:S(2)}) copy-start(bf16[1,2,32,256]{3,2,1,0:T(8,128)(2,1)} %copy.74) | copy-start | bytes 98308
  353.8 22.2 %copy-start.34 = (bf16[1,2,32,256]{3,2,1,0:T(8,128)(2,1)S(1)}, bf16[1,2,32,256]{3,2,1,0:T(8,128)(2,1)}, u32[]{:S(2)}) copy-start(bf16[1,2,32,256]{3,2,1,0:T(8,128)(2,1)} %copy.75) | copy-start | bytes 98308
  353.8 22.8 %copy-start.33 = (bf16[1,2,32,256]{3,2,1,0:T(8,128)(2,1)S(1)}, bf16[1,2,32,256]{3,2,1,0:T(8,128)(2,1)}, u32[]{:S(2)}) copy-start(bf16[1,2,32,256]{3,2,1,0:T(8,128)(2,1)} %copy.76) | copy-start | bytes 98308
  353.9 23.3 %copy-start.32 = (bf16[1,2,32,256]{3,2,1,0:T(8,128)(2,1)S(1)}, bf16[1,2,32,256]{3,2,1,0:T(8,128)(2,1)}, u32[]{:S(2)}) copy-start(bf16[1,2,32,256]{3,2,1,0:T(8,128)(2,1)} %copy.77) | copy-start | bytes 98308
  353.9 23.9 %copy-start.31 = (bf16[1,2,32,256]{3,2,1,0:T(8,128)(2,1)S(1)}, bf16[1,2,32,256]{3,2,1,0:T(8,128)(2,1)}, u32[]{:S(2)}) copy-start(bf16[1,2,32,256]{3,2,1,0:T(8,128)(2,1)} %copy.78) | copy-start | bytes 98308
  354.0 24.4 %copy-start.30 = (bf16[1,2,32,256]{3,2,1,0:T(8,128)(2,1)S(1)}, bf16[1,2,32,256]{3,2,1,0:T(8,128)(2,1)}, u32[]{:S(2)}) copy-start(bf16[1,2,32,256]{3,2,1,0:T(8,128)(2,1)} %copy.79) | copy-start | bytes 98308
  354.0 25.0 %copy-start.29 = (bf16[1,2,32,256]{3,2,1,0:T(8,128)(2,1)S(1)}, bf16[1,2,32,256]{3,2,1,0:T(8,128)(2,1)}, u32[]{:S(2)}) copy-start(bf16[1,2,32,256]{3,2,1,0:T(8,128)(2,1)} %copy.80) | copy-start | bytes 98308
  354.0 25.6 %copy-start.28 = (bf16[1,2,32,256]{3,2,1,0:T(8,128)(2,1)S(1)}, bf16[1,2,32,256]{3,2,1,0:T(8,128)(2,1)}, u32[]{:S(2)}) copy-start(bf16[1,2,32,256]{3,2,1,0:T(8,128)(2,1)} %copy.81) | copy-start | bytes 98308
  354.1 26.1 %copy-start.27 = (bf16[1,2,32,256]{3,2,1,0:T(8,128)(2,1)S(1)}, bf16[1,2,32,256]{3,2,1,0:T(8,128)(2,1)}, u32[]{:S(2)}) copy-start(bf16[1,2,32,256]{3,2,1,0:T(8,128)(2,1)} %copy.82) | copy-start | bytes 98308
  354.1 26.7 %copy-start.26 = (bf16[1,2,32,256]{3,2,1,0:T(8,128)(2,1)S(1)}, bf16[1,2,32,256]{3,2,1,0:T(8,128)(2,1)}, u32[]{:S(2)}) copy-start(bf16[1,2,32,256]{3,2,1,0:T(8,128)(2,1)} %copy.83) | copy-start | bytes 98308
  355.1 42.1 %copy-start.25 = (bf16[1,2,32,256]{3,2,1,0:T(8,128)(2,1)S(1)}, bf16[1,2,32,256]{3,2,1,0:T(8,128)(2,1)}, u32[]{:S(2)}) copy-start(bf16[1,2,32,256]{3,2,1,0:T(8,128)(2,1)} %copy.110) | copy-start | bytes 98308
  355.2 42.6 %copy-start.24 = (bf16[1,2,32,256]{3,2,1,0:T(8,128)(2,1)S(1)}, bf16[1,2,32,256]{3,2,1,0:T(8,128)(2,1)}, u32[]{:S(2)}) copy-start(bf16[1,2,32,256]{3,2,1,0:T(8,128)(2,1)} %copy.111) | copy-start | bytes 98308
  355.3 43.2 %copy-start.23 = (bf16[1,2,32,256]{3,2,1,0:T(8,128)(2,1)S(1)}, bf16[1,2,32,256]{3,2,1,0:T(8,128)(2,1)}, u32[]{:S(2)}) copy-start(bf16[1,2,32,256]{3,2,1,0:T(8,128)(2,1)} %copy.112) | copy-start | bytes 98308
  355.3 43.8 %copy-start.22 = (bf16[1,2,32,256]{3,2,1,0:T(8,128)(2,1)S(1)}, bf16[1,2,32,256]{3,2,1,0:T(8,128)(2,1)}, u32[]{:S(2)}) copy-start(bf16[1,2,32,256]{3,2,1,0:T(8,128)(2,1)} %copy.113) | copy-start | bytes 98308
  355.3 44.4 %copy-start.21 = (bf16[1,2,32,256]{3,2,1,0:T(8,128)(2,1)S(1)}, bf16[1,2,32,256]{3,2,1,0:T(8,128)(2,1)}, u32[]{:S(2)}) copy-start(bf16[1,2,32,256]{3,2,1,0:T(8,128)(2,1)} %copy.114) | copy-start | bytes 98308
  355.4 44.9 %copy-start.20 = (bf16[1,2,32,256]{3,2,1,0:T(8,128)(2,1)S(1)}, bf16[1,2,32,256]{3,2,1,0:T(8,128)(2,1)}, u32[]{:S(2)}) copy-start(bf16[1,2,32,256]{3,2,1,0:T(8,128)(2,1)} %copy.115) | copy-start | bytes 98308
  355.4 45.5 %copy-start.19 = (bf16[1,2,32,256]{3,2,1,0:T(8,128)(2,1)S(1)}, bf16[1,2,32,256]{3,2,1,0:T(8,128)(2,1)}, u32[]{:S(2)}) copy-start(bf16[1,2,32,256]{3,2,1,0:T(8,128)(2,1)} %copy.116) | copy-start | bytes 98308
  355.5 46.0 %copy-start.18 = (bf16[1,2,32,256]{3,2,1,0:T(8,128)(2,1)S(1)}, bf16[1,2,32,256]{3,2,1,0:T(8,128)(2,1)}, u32[]{:S(2)}) copy-start(bf16[1,2,32,256]{3,2,1,0:T(8,128)(2,1)} %copy.117) | copy-start | bytes 98308
  355.5 46.6 %copy-start.17 = (bf16[1,2,32,256]{3,2,1,0:T(8,128)(2,1)S(1)}, bf16[1,2,32,256]{3,2,1,0:T(8,128)(2,1)}, u32[]{:S(2)}) copy-start(bf16[1,2,32,256]{3,2,1,0:T(8,128)(2,1)} %copy.118) | copy-start | bytes 98308
  355.5 47.2 %copy-start.16 = (bf16[1,2,32,256]{3,2,1,0:T(8,128)(2,1)S(1)}, bf16[1,2,32,256]{3,2,1,0:T(8,128)(2,1)}, u32[]{:S(2)}) copy-start(bf16[1,2,32,256]{3,2,1,0:T(8,128)(2,1)} %copy.119) | copy-start | bytes 98308
  355.6 47.7 %copy-start.15 = (bf16[1,2,32,256]{3,2,1,0:T(8,128)(2,1)S(1)}, bf16[1,2,32,256]{3,2,1,0:T(8,128)(2,1)}, u32[]{:S(2)}) copy-start(bf16[1,2,32,256]{3,2,1,0:T(8,128)(2,1)} %copy.120) | copy-start | bytes 98308
  355.6 48.3 %copy-start.14 = (bf16[1,2,32,256]{3,2,1,0:T(8,128)(2,1)S(1)}, bf16[1,2,32,256]{3,2,1,0:T(8,128)(2,1)}, u32[]{:S(2)}) copy-start(bf16[1,2,32,256]{3,2,1,0:T(8,128)(2,1)} %copy.121) | copy-start | bytes 98308
  404.5 56.4 %all-to-all-start.4 = ((bf16[64,2,32,256]{3,2,1,0:T(8,128)(2,1)}), bf16[64,2,32,256]{3,2,1,0:T(8,128)(2,1)S(1)}, u32[]{:S(2)}, u32[]{:S(2)}) async-start(bf16[64,2,32,256]{3,2,1,0:T(8,128)(2,1)} %constant_dynamic-update-slice_fusion), calls=%async_computation.4 | async-start | bytes 4194304 | tf_op jit(solution)/shard_map/all_to_all | solution.py:57
  (12 other events, 71.5 us)
